TPU v7x, 32 devices: a whole 2x2x4 slice. The times are simulated.
32 devices in a mesh: rep: 4 (over y, core), exp: 8 (over z, x).
Axes of the slice: x: 2, y: 2, z: 4, core: 2. Of those that a mesh axis runs over, the one named last changes fastest.
Arguments:
- tokens: bfloat16 [8192, 1024], P(('rep', 'exp')), may hold values from -6 to 6
- cotangent: bfloat16 [8192, 1024], P(('rep', 'exp')), may hold values from -6 to 6
- expert_ids: int32 [8192, 8], P(('rep', 'exp')), may hold values from 0 to 15, as said below
- combine: bfloat16 [8192, 8], P(('rep', 'exp')), may hold values from 0.049804688 to 0.34960938
- gate_weight: bfloat16 [4, 16, 1024, 384], P('rep', 'exp'), may hold values from -0.1875 to 0.1875
- up_weight: bfloat16 [4, 16, 1024, 384], P('rep', 'exp'), may hold values from -0.1875 to 0.1875
- down_weight: bfloat16 [4, 16, 384, 1024], P('rep', 'exp'), may hold values from -0.625 to 0.625
- moment1: float32 [4, 16, 384, 1024], P('rep', 'exp'), may hold values from -4 to 4
- moment2: float32 [4, 16, 384, 1024], P('rep', 'exp'), may hold values from 0.01 to 1
- round_k: int32 [8], P('exp'), may hold values from 0 to 1
Outputs:
- mixed: bfloat16 [8192, 1024], P(('rep', 'exp'))
- input_grad: bfloat16 [8192, 1024], P(('rep', 'exp'))
- gate_grad: bfloat16 [4, 16, 1024, 384], P('rep', 'exp')
- up_grad: bfloat16 [4, 16, 1024, 384], P('rep', 'exp')
- new_down: bfloat16 [4, 16, 384, 1024], P('rep', 'exp')
- new_moment1: float32 [4, 16, 384, 1024], P('rep', 'exp')
- new_moment2: float32 [4, 16, 384, 1024], P('rep', 'exp')
Inputs may be any that keep to these rules, and one draw needn't show every extreme that they name: `expert_ids`: each row names 8 different experts. Of the 256 rows of one device, at most 256 name any one expert, and at most 384 name one of the two experts 2i and 2i + 1; in every draw one expert is named by exactly 256 rows of every device, and one such pair of experts by exactly 384.
All inputs are finite; a program needn't handle non-finite values.
Results may differ from a plain program's by a relative error of at most 0.0064.
Values may be sent and summed in bfloat16 or wider, within the bound.
No kernel may reach another device: no remote copies, remote signals or barrier semaphores. Data moves between devices by JAX's collectives and lax.ppermute only.
A program may use at most 192 MiB of HBM per device.

v0:
```python
import jax
import jax.numpy as jnp
from jax import lax
from jax.sharding import PartitionSpec as P

ROUNDS = 2
CHUNK_ROWS = 2048
beta_one = 0.9
beta_two = 0.999
learn_rate = 0.01
decay_rate = 0.1
adam_eps = 1e-08
step_count = 100.0


def shifted(value, axis, by):
    size = lax.axis_size(axis)
    return lax.ppermute(value, axis, [(i, (i + by) % size) for i in range(size)])


def dense_weights(expert_ids, combine, experts):
    expert_iota = jnp.arange(experts, dtype=jnp.int32)
    hit = expert_ids[:, :, None] == expert_iota[None, None, :]
    picked = jnp.where(hit, combine.astype(jnp.float32)[:, :, None], 0.0)
    return jnp.sum(picked, axis=1).astype(jnp.bfloat16)


def per_device(
    tokens,
    cotangent,
    expert_ids,
    combine,
    gate_weight,
    up_weight,
    down_weight,
    moment1,
    moment2,
    round_k,
):
    local_experts = gate_weight.shape[1]
    devices_exp = lax.axis_size("exp")
    experts = local_experts * devices_exp
    my_exp = lax.axis_index("exp")
    weight_table = dense_weights(expert_ids, combine, experts)
    group_weight = lax.all_gather(weight_table, "exp", axis=0, tiled=True)
    group_tokens = lax.all_gather(tokens, "exp", axis=0, tiled=True)
    group_cot = lax.all_gather(cotangent, "exp", axis=0, tiled=True)
    local_weight = lax.dynamic_slice_in_dim(
        group_weight, my_exp * local_experts, local_experts, axis=1
    ).astype(jnp.float32)
    local_weight = jnp.transpose(local_weight)[:, :, None]
    gate_matrix = gate_weight[0]
    up_matrix = up_weight[0]
    down_matrix = down_weight[0]

    def chunk_pass(chunk_tokens, chunk_cot, chunk_weight):
        gate_value = jnp.einsum(
            "td,edh->eth", chunk_tokens, gate_matrix, preferred_element_type=jnp.float32
        )
        up_value = jnp.einsum(
            "td,edh->eth", chunk_tokens, up_matrix, preferred_element_type=jnp.float32
        )
        sigmoid_gate = jax.nn.sigmoid(gate_value)
        active = gate_value * sigmoid_gate
        hidden = (active * up_value).astype(jnp.bfloat16)
        expert_out = jnp.einsum(
            "eth,ehd->etd", hidden, down_matrix, preferred_element_type=jnp.float32
        ).astype(jnp.bfloat16)
        mixed_part = jnp.sum(chunk_weight * expert_out.astype(jnp.float32), axis=0)
        slot_cot = (chunk_weight * chunk_cot.astype(jnp.float32)[None]).astype(jnp.bfloat16)
        hidden_cot = jnp.einsum(
            "etd,ehd->eth", slot_cot, down_matrix, preferred_element_type=jnp.float32
        )
        gate_cot = (
            hidden_cot * up_value * sigmoid_gate * (1.0 + gate_value * (1.0 - sigmoid_gate))
        ).astype(jnp.bfloat16)
        up_cot = (hidden_cot * active).astype(jnp.bfloat16)
        down_grad = jnp.einsum("eth,etd->ehd", hidden, slot_cot, preferred_element_type=jnp.float32)
        gate_grad = jnp.einsum(
            "td,eth->edh", chunk_tokens, gate_cot, preferred_element_type=jnp.float32
        )
        up_grad = jnp.einsum(
            "td,eth->edh", chunk_tokens, up_cot, preferred_element_type=jnp.float32
        )
        input_cot = (
            jnp.einsum("eth,edh->etd", gate_cot, gate_matrix, preferred_element_type=jnp.float32)
            + jnp.einsum("eth,edh->etd", up_cot, up_matrix, preferred_element_type=jnp.float32)
        ).astype(jnp.bfloat16)
        input_part = jnp.sum(input_cot.astype(jnp.float32), axis=0)
        return (mixed_part, input_part, gate_grad, up_grad, down_grad)

    group_count = group_tokens.shape[0]
    chunk = min(group_count, CHUNK_ROWS)
    chunks = group_count // chunk
    if chunks == 1:
        mixed_part, input_part, gate_grad, up_grad, down_grad = chunk_pass(
            group_tokens, group_cot, local_weight
        )
    else:

        def step(carry, packed):
            parts = chunk_pass(*packed)
            grads = tuple((acc + part for acc, part in zip(carry, parts[2:])))
            return (grads, parts[:2])

        zeros = (
            jnp.zeros(gate_matrix.shape, jnp.float32),
            jnp.zeros(up_matrix.shape, jnp.float32),
            jnp.zeros(down_matrix.shape, jnp.float32),
        )
        packed = (
            group_tokens.reshape(chunks, chunk, -1),
            group_cot.reshape(chunks, chunk, -1),
            jnp.transpose(local_weight.reshape(local_experts, chunks, chunk, 1), (1, 0, 2, 3)),
        )
        (gate_grad, up_grad, down_grad), (mixed_parts, input_parts) = lax.scan(step, zeros, packed)
        mixed_part = mixed_parts.reshape(group_count, -1)
        input_part = input_parts.reshape(group_count, -1)
    gate_grad = gate_grad.astype(jnp.bfloat16)
    up_grad = up_grad.astype(jnp.bfloat16)
    mixed = lax.psum_scatter(mixed_part, "exp", scatter_dimension=0, tiled=True).astype(
        jnp.bfloat16
    )
    input_grad = lax.psum_scatter(input_part, "exp", scatter_dimension=0, tiled=True).astype(
        jnp.bfloat16
    )
    peers = [shifted(down_weight, "rep", 1 << bit_index) for bit_index in range(ROUNDS)]
    peer_down = peers[0]
    for bit_index in range(1, ROUNDS):
        peer_down = jnp.where(round_k[0] == bit_index, peers[bit_index], peer_down)
    bias_one = 1.0 - beta_one**step_count
    bias_two = 1.0 - beta_two**step_count
    first = beta_one * moment1[0] + (1.0 - beta_one) * down_grad
    second = beta_two * moment2[0] + (1.0 - beta_two) * down_grad * down_grad
    own_down = down_matrix.astype(jnp.float32)
    averaged = (own_down + peer_down[0].astype(jnp.float32)) * 0.5
    update = first / bias_one / (jnp.sqrt(second / bias_two) + adam_eps)
    new_down = (averaged - learn_rate * (update + decay_rate * own_down)).astype(jnp.bfloat16)
    return (
        mixed,
        input_grad,
        gate_grad[None],
        up_grad[None],
        new_down[None],
        first[None],
        second[None],
    )


def solution(mesh):
    return jax.shard_map(
        per_device,
        mesh=mesh,
        in_specs=(
            P(("rep", "exp"), None),
            P(("rep", "exp"), None),
            P(("rep", "exp"), None),
            P(("rep", "exp"), None),
            P("rep", "exp", None, None),
            P("rep", "exp", None, None),
            P("rep", "exp", None, None),
            P("rep", "exp", None, None),
            P("rep", "exp", None, None),
            P("exp"),
        ),
        out_specs=(
            P(("rep", "exp"), None),
            P(("rep", "exp"), None),
            P("rep", "exp", None, None),
            P("rep", "exp", None, None),
            P("rep", "exp", None, None),
            P("rep", "exp", None, None),
            P("rep", "exp", None, None),
        ),
        check_vma=False,
    )
```

profile of v0, /device:TPU:0, one launch (start us, length us, event | category | flops | bytes accessed | tf_op | source)
XLA Modules:
  0.0 505.3 jit_solution(15658487517615227164)
XLA Ops:
  9.4 0.7 select_reduce_fusion
  10.1 32.6 %all_gather.9 = bf16[2048,16]{0,1:T(8,128)(2,1)S(1)} all-gather(bf16[256,16]{0,1:T(8,128)(2,1)S(1)} %select_reduce_fusion), channel_id=1, replica_groups=mesh['rep'=4,'exp'=8] {'exp'}, dimensions={0}, use_global_device_ids=true | all-gather | bytes 73728 | tf_op jit(solution)/shard_map/all_gather | solution.py:45
  42.8 43.9 %all-gather.5.cloned.1.call-done = bf16[2048,1024]{1,0:T(8,128)(2,1)} async-done(((bf16[256,1024]{1,0:T(8,128)(2,1)}), bf16[2048,1024]{1,0:T(8,128)(2,1)}) %all-gather.5.cloned.1.call-update) | async-done | bytes 4194320 | tf_op jit(solution)/shard_map/all_gather | solution.py:47
  86.7 6.5 %convert_element_type.70 = f32[2048,1024]{1,0:T(8,128)} convert(bf16[2048,1024]{1,0:T(8,128)(2,1)} %all-gather.5.cloned.1.call-done) | non-fusion elementwise | flops 2097152 | bytes 12582912 | tf_op jit(solution)/shard_map/convert_element_type | solution.py:70
  93.1 67.4 %all-gather.3.cloned.1.call-done = bf16[2048,1024]{1,0:T(8,128)(2,1)} async-done(((bf16[256,1024]{1,0:T(8,128)(2,1)}), bf16[2048,1024]{1,0:T(8,128)(2,1)}) %all-gather.3.cloned.1.call-update) | async-done | bytes 4194320 | tf_op jit(solution)/shard_map/all_gather | solution.py:46
  160.5 7.7 %fusion.18 = f32[2,384,2048]{2,1,0:T(8,128)} fusion(bf16[2048,1024]{1,0:T(8,128)(2,1)} %all-gather.3.cloned.1.call-done, bf16[1,2,1024,384]{3,2,1,0:T(8,128)(2,1)S(1)} %copy-done.3), kind=kOutput, calls=%fused_computation.29 | convolution fusion | flops 3221225472 | bytes 12058624 | tf_op jit(solution)/shard_map/td,edh->eth/dot_general | solution.py:60
  168.2 5.5 %fusion.20 = f32[2,384,2048]{2,1,0:T(8,128)} fusion(bf16[2048,1024]{1,0:T(8,128)(2,1)S(1)} %copy-done.4, bf16[1,2,1024,384]{3,2,1,0:T(8,128)(2,1)S(1)} %copy-done), kind=kOutput, calls=%fused_computation.31 | convolution fusion | flops 3221225472 | bytes 12058624 | tf_op jit(solution)/shard_map/td,edh->eth/dot_general | solution.py:57
  173.7 12.6 %multiply_convert_fusion.3 = (bf16[2,2048,384]{1,2,0:T(8,128)(2,1)}, bf16[2,2048,384]{1,2,0:T(8,128)(2,1)}, bf16[2,2048,384]{1,2,0:T(8,128)(2,1)}) fusion(f32[2,384,2048]{2,1,0:T(8,128)} %fusion.20, f32[2,384,2048]{2,1,0:T(8,128)} %fusion.18, bf16[1,2,384,1024]{3,2,1,0:T(8,128)(2,1)S(1)} %copy-done.5, f32[2048,1024]{1,0:T(8,128)} %convert_element_type.70, ...), kind=kOutput, calls=%fused_computation.23 | convolution fusion | flops 3253207040 | bytes 31997952 | tf_op jit(solution)/shard_map/etd,ehd->eth/dot_general | solution.py:71
  186.3 10.9 %multiply_reduce_fusion = f32[2048,1024]{1,0:T(8,128)} fusion(f32[2,2048]{1,0:T(2,128)S(1)} %convert_bitcast_fusion, bf16[2,2048,384]{1,2,0:T(8,128)(2,1)} %get-tuple-element.23, bf16[1,2,384,1024]{3,2,1,0:T(8,128)(2,1)S(1)} %copy-done.5), kind=kOutput, calls=%fused_computation.3 | convolution fusion | flops 3235905536 | bytes 13123584 | tf_op jit(solution)/shard_map/eth,ehd->etd/dot_general | solution.py:66
  197.4 11.0 %fusion.38 = f32[2,2048,1024]{2,1,0:T(8,128)} fusion(bf16[2,2048,384]{1,2,0:T(8,128)(2,1)} %get-tuple-element.22, bf16[1,2,1024,384]{3,2,1,0:T(8,128)(2,1)S(1)} %copy-done), kind=kOutput, calls=%fused_computation.48 | convolution fusion | flops 3221225472 | bytes 21495808 | tf_op jit(solution)/shard_map/eth,edh->etd/dot_general | solution.py:86
  208.3 12.9 %convert_reduce_fusion = f32[2048,1024]{1,0:T(8,128)} fusion(f32[2,2048,1024]{2,1,0:T(8,128)} %fusion.38, bf16[2,2048,384]{1,2,0:T(8,128)(2,1)S(1)} %copy-done.2, bf16[1,2,1024,384]{3,2,1,0:T(8,128)(2,1)S(1)} %copy-done.3), kind=kOutput, calls=%fused_computation | convolution fusion | flops 3235905536 | bytes 29884416 | tf_op jit(solution)/shard_map/eth,edh->etd/dot_general | solution.py:87
  221.3 1.4 copy-done.6
  222.7 1.5 collective-permute-start
  224.9 6.6 %fusion.45 = bf16[1,2,1024,384]{2,3,1,0:T(8,128)(2,1)S(1)} fusion(bf16[2,2048,384]{1,2,0:T(8,128)(2,1)} %get-tuple-element.22, bf16[2048,1024]{1,0:T(8,128)(2,1)} %all-gather.3.cloned.1.call-done), kind=kOutput, calls=%fused_computation.53 | convolution fusion | flops 3222011904 | bytes 8912896 | tf_op jit(solution)/shard_map/td,eth->edh/dot_general | solution.py:79
  231.5 1.6 copy.35
  233.1 6.7 %fusion.42 = bf16[1,2,1024,384]{2,3,1,0:T(8,128)(2,1)S(1)} fusion(bf16[2,2048,384]{1,2,0:T(8,128)(2,1)} %get-tuple-element.21, bf16[2048,1024]{1,0:T(8,128)(2,1)} %all-gather.3.cloned.1.call-done), kind=kOutput, calls=%fused_computation.52 | convolution fusion | flops 3222011904 | bytes 8912896 | tf_op jit(solution)/shard_map/td,eth->edh/dot_general | solution.py:82
  239.8 1.6 copy.36
  241.4 17.6 %collective-permute-done.1 = bf16[1,2,384,1024]{3,2,1,0:T(8,128)(2,1)} collective-permute-done((bf16[1,2,384,1024]{3,2,1,0:T(8,128)(2,1)S(1)}, bf16[1,2,384,1024]{3,2,1,0:T(8,128)(2,1)}, u32[]{:S(2)}, u32[]{:S(2)}) %collective-permute-start.1) | collective-permute-done | bytes 1572896 | tf_op jit(solution)/shard_map/ppermute | solution.py:18
  259.0 1.1 collective-permute-done
  260.1 15.9 %fusion.49 = (f32[1,2,384,1024]{3,2,1,0:T(8,128)}, bf16[1,2,384,1024]{3,2,1,0:T(8,128)(2,1)}, f32[1,2,384,1024]{3,2,1,0:T(8,128)}) fusion(f32[1,2,384,1024]{3,2,1,0:T(8,128)} %param.18, f32[1,2,384,1024]{3,2,1,0:T(8,128)} %param.17, bf16[1,2,384,1024]{3,2,1,0:T(8,128)(2,1)} %collective-permute-done, bf16[1,2,384,1024]{3,2,1,0:T(8,128)(2,1)} %collective-permute-done.1, ...), kind=kOutput, calls=%fused_computation.55 | convolution fusion | flops 3246129152 | bytes 30425088 | tf_op jit(solution)/shard_map/eth,etd->ehd/dot_general | solution.py:78
  276.0 68.6 %reduce-scatter.3.cloned.1.call-done = f32[256,1024]{1,0:T(8,128)} async-done(((f32[2048,1024]{1,0:T(8,128)}), f32[256,1024]{1,0:T(8,128)}) %reduce-scatter.3.cloned.1.call-update) | async-done | bytes 1048592 | tf_op jit(solution)/shard_map/reduce_scatter | solution.py:121
  344.6 2.1 convert_element_type.69
  346.7 149.9 %reduce-scatter.5.cloned.1.call-done = f32[256,1024]{1,0:T(8,128)} async-done(((f32[2048,1024]{1,0:T(8,128)}), f32[256,1024]{1,0:T(8,128)}) %reduce-scatter.5.cloned.1.call-update) | async-done | bytes 1048592 | tf_op jit(solution)/shard_map/reduce_scatter | solution.py:124
  496.6 2.1 convert_element_type.76
  (24 shorter events, 2.5 us)
Async XLA Ops:
  7.2 161.0 %copy-start = (bf16[1,2,1024,384]{3,2,1,0:T(8,128)(2,1)S(1)}, bf16[1,2,1024,384]{3,2,1,0:T(8,128)(2,1)}, u32[]{:S(2)}) copy-start(bf16[1,2,1024,384]{3,2,1,0:T(8,128)(2,1)} %param.14) | copy-start | bytes 4718596
  7.2 79.5 %all-gather.5.cloned.1.call-start = ((), (), s32[]{:S(2)}) async-start(), calls=%async_computation.4 | async-start | bytes 4718592 | tf_op jit(solution)/shard_map/all_gather | solution.py:47
  7.9 152.6 %all-gather.3.cloned.1.call-start = ((), (), s32[]{:S(2)}) async-start(), calls=%async_computation.2 | async-start | bytes 4718592 | tf_op jit(solution)/shard_map/all_gather | solution.py:46
  8.7 336.0 %reduce-scatter.3.cloned.1.call-start = ((), (), s32[]{:S(2)}) async-start(), calls=%async_computation.3 | async-start | bytes 9437184 | tf_op jit(solution)/shard_map/reduce_scatter | solution.py:121
  42.8 117.7 %copy-start.3 = (bf16[1,2,1024,384]{3,2,1,0:T(8,128)(2,1)S(1)}, bf16[1,2,1024,384]{3,2,1,0:T(8,128)(2,1)}, u32[]{:S(2)}) copy-start(bf16[1,2,1024,384]{3,2,1,0:T(8,128)(2,1)} %param.15) | copy-start | bytes 4718596
  160.5 7.7 %copy-start.4 = (bf16[2048,1024]{1,0:T(8,128)(2,1)S(1)}, bf16[2048,1024]{1,0:T(8,128)(2,1)}, u32[]{:S(2)}) copy-start(bf16[2048,1024]{1,0:T(8,128)(2,1)} %all-gather.3.cloned.1.call-done) | copy-start | bytes 12582916
  168.2 5.5 %copy-start.5 = (bf16[1,2,384,1024]{3,2,1,0:T(8,128)(2,1)S(1)}, bf16[1,2,384,1024]{3,2,1,0:T(8,128)(2,1)}, u32[]{:S(2)}) copy-start(bf16[1,2,384,1024]{3,2,1,0:T(8,128)(2,1)} %param.16) | copy-start | bytes 4718596
  197.1 299.5 %reduce-scatter.5.cloned.1.call-start = ((), (), s32[]{:S(2)}) async-start(), calls=%async_computation.5 | async-start | bytes 9437184 | tf_op jit(solution)/shard_map/reduce_scatter | solution.py:124
  197.4 11.0 %copy-start.2 = (bf16[2,2048,384]{1,2,0:T(8,128)(2,1)S(1)}, bf16[2,2048,384]{1,2,0:T(8,128)(2,1)}, u32[]{:S(2)}) copy-start(bf16[2,2048,384]{1,2,0:T(8,128)(2,1)} %get-tuple-element.21) | copy-start | bytes 9437188
  221.3 1.4 copy-start.6
  222.7 36.2 %collective-permute-start.1 = (bf16[1,2,384,1024]{3,2,1,0:T(8,128)(2,1)S(1)}, bf16[1,2,384,1024]{3,2,1,0:T(8,128)(2,1)}, u32[]{:S(2)}, u32[]{:S(2)}) collective-permute-start(bf16[1,2,384,1024]{3,2,1,0:T(8,128)(2,1)S(1)} %copy-done.6), channel_id=1, source_target_pairs={{0,8},{8,16},{16,24},{24,0},{1,9},{9,17},{17,25},{25,1},{2,10},{10... | collective-permute-start | bytes 4718600 | tf_op jit(solution)/shard_map/ppermute | solution.py:18
  222.7 37.3 %collective-permute-start = (bf16[1,2,384,1024]{3,2,1,0:T(8,128)(2,1)S(1)}, bf16[1,2,384,1024]{3,2,1,0:T(8,128)(2,1)}, u32[]{:S(2)}, u32[]{:S(2)}) collective-permute-start(bf16[1,2,384,1024]{3,2,1,0:T(8,128)(2,1)S(1)} %copy-done.6), channel_id=1, source_target_pairs={{0,16},{8,24},{16,0},{24,8},{1,17},{9,25},{17,1},{25,9},{2,18},{10... | collective-permute-start | bytes 4718600 | tf_op jit(solution)/shard_map/ppermute | solution.py:18
  260.1 238.7 %copy-start.1 = (bf16[1,2,1024,384]{3,2,1,0:T(8,128)(2,1)S(1)}, bf16[1,2,1024,384]{3,2,1,0:T(8,128)(2,1)}, u32[]{:S(2)}) copy-start(bf16[1,2,1024,384]{3,2,1,0:T(8,128)(2,1)} %param.14) | copy-start | bytes 4718596
Sparse Core Ops, SparseCore 0:
  10.1 76.4 all-gather.4
  88.8 71.6 all-gather.2
  197.3 147.3 reduce-scatter.2
  348.5 148.0 reduce-scatter.4
where the time goes:
time: 506 us; the launch traced here: 505 us
  waiting for transfers between devices  350 us (69%)
  matrix products  89.8 us (18%)
  blocking collectives  32.6 us (6%)
  between operations  14.5 us (3%)
  other arithmetic  12.1 us (2%)
    reduce_scatter x1, waiting for transfers between devices, per_device(): lax.psum_scatter(input_part, 'exp', scatter_dimension=0, tiled=True)  150 us
    reduce_scatter x1, waiting for transfers between devices, per_device(): lax.psum_scatter(mixed_part, 'exp', scatter_dimension=0, tiled=True)  68.6 us
    all_gather x1, waiting for transfers between devices, per_device(): group_tokens = lax.all_gather(tokens, 'exp', axis=0, tiled=True)  67.4 us
    all_gather x1, waiting for transfers between devices, per_device(): group_cot = lax.all_gather(cotangent, 'exp', axis=0, tiled=True)  43.9 us
    all_gather x1, blocking collectives, per_device(): group_weight = lax.all_gather(weight_table, 'exp', axis=0, tiled=True)  32.6 us
    ppermute x2, waiting for transfers between devices, shifted(): lax.ppermute(value, axis, [(i, (i + by) % size) for i in range(size)])  18.7 us
    dot_general x1, matrix products, chunk_pass(): jnp.einsum('eth,etd->ehd', hidden, slot_cot, preferred_element_type=jnp.f...  15.9 us
    dot_general x1, matrix products, chunk_pass(): jnp.einsum('eth,edh->etd', up_cot, up_matrix, preferred_element_type=jnp....  12.9 us
  transfers between devices with their start and end apart: 6, of which 6 were waited for; matrix products, arithmetic and copies ran while one was open for 13% of the time, Pallas kernels for 0%

commit v1 on v0

--- a/solution.py
+++ b/solution.py
@@ -43,8 +43,11 @@
     my_exp = lax.axis_index("exp")
     weight_table = dense_weights(expert_ids, combine, experts)
     group_weight = lax.all_gather(weight_table, "exp", axis=0, tiled=True)
-    group_tokens = lax.all_gather(tokens, "exp", axis=0, tiled=True)
-    group_cot = lax.all_gather(cotangent, "exp", axis=0, tiled=True)
+    group_tokens, group_cot = jnp.split(
+        lax.all_gather(jnp.concatenate([tokens, cotangent], axis=1), "exp", axis=0, tiled=True),
+        [tokens.shape[1]],
+        axis=1,
+    )
     local_weight = lax.dynamic_slice_in_dim(
         group_weight, my_exp * local_experts, local_experts, axis=1
     ).astype(jnp.float32)

time: 506 us -> 484 us (0.957)
  waiting for transfers between devices: 350 us -> 333 us
  matrix products: 89.8 us -> 84.1 us
    all_gather x2 -> x1, waiting for transfers between devices: 111 us -> 96.2 us  [per_device(): lax.all_gather(jnp.concatenate([tokens, cotangent], axis=1), 'exp', axis=...]
  transfers between devices with their start and end apart: 6 -> 5, of which waited for: 6 -> 5; matrix products, arithmetic and copies ran while one was open for 13% -> 12% of each run, Pallas kernels for 0% -> 0%
where the time goes in v1:
time: 484 us
  waiting for transfers between devices  333 us (69%)
  matrix products  84.1 us (17%)
  blocking collectives  32.7 us (7%)
  between operations  14.5 us (3%)
  other arithmetic  9.97 us (2%)
  local copies, waits for them, and re-layouts  7.7 us (2%)
    reduce_scatter x1, waiting for transfers between devices, per_device(): lax.psum_scatter(input_part, 'exp', scatter_dimension=0, tiled=True)  150 us
    all_gather x1, waiting for transfers between devices, per_device(): lax.all_gather(jnp.concatenate([tokens, cotangent], axis=1), 'exp', axis=...  96.2 us
    reduce_scatter x1, waiting for transfers between devices, per_device(): lax.psum_scatter(mixed_part, 'exp', scatter_dimension=0, tiled=True)  68.5 us
    all_gather x1, blocking collectives, per_device(): group_weight = lax.all_gather(weight_table, 'exp', axis=0, tiled=True)  32.7 us
    ppermute x2, waiting for transfers between devices, shifted(): lax.ppermute(value, axis, [(i, (i + by) % size) for i in range(size)])  18.4 us
    dot_general x1, matrix products, chunk_pass(): jnp.einsum('eth,etd->ehd', hidden, slot_cot, preferred_element_type=jnp.f...  16.2 us
    dot_general x1, matrix products, chunk_pass(): jnp.einsum('eth,edh->etd', up_cot, up_matrix, preferred_element_type=jnp....  13.2 us
    dot_general x1, matrix products, chunk_pass(): jnp.einsum('etd,ehd->eth', slot_cot, down_matrix, preferred_element_type=...  11.8 us
  transfers between devices with their start and end apart: 5, of which 5 were waited for; matrix products, arithmetic and copies ran while one was open for 12% of the time, Pallas kernels for 0%

profile of v1, /device:TPU:0, one launch (start us, length us, event | category | flops | bytes accessed | tf_op | source)
XLA Modules:
  0.0 484.0 jit_solution(8828539699161372524)
XLA Ops:
  7.3 2.4 pad_maximum_fusion
  9.8 32.7 %all_gather.6 = bf16[2048,16]{0,1:T(8,128)(2,1)S(1)} all-gather(bf16[256,16]{0,1:T(8,128)(2,1)S(1)} %select_reduce_fusion), channel_id=1, replica_groups=mesh['rep'=4,'exp'=8] {'exp'}, dimensions={0}, use_global_device_ids=true | all-gather | bytes 73728 | tf_op jit(solution)/shard_map/all_gather | solution.py:45
  42.5 96.2 %all-gather.2.cloned.1.call-done = bf16[2048,2048]{1,0:T(8,128)(2,1)} async-done(((bf16[256,2048]{1,0:T(8,128)(2,1)}), bf16[2048,2048]{1,0:T(8,128)(2,1)}) %all-gather.2.cloned.1.call-update) | async-done | bytes 8388624 | tf_op jit(solution)/shard_map/all_gather | solution.py:47
  138.7 3.4 slice_convert_fusion
  142.1 1.2 copy-done.3
  143.3 5.2 %fusion.23 = f32[2048,2,384]{2,0,1:T(8,128)} fusion(bf16[1,2,1024,384]{3,2,1,0:T(8,128)(2,1)S(1)} %copy-done.4, bf16[2048,2048]{1,0:T(8,128)(2,1)S(1)} %copy-done.3), kind=kOutput, calls=%fused_computation.41 | convolution fusion | flops 3221225472 | bytes 12058624 | tf_op jit(solution)/shard_map/td,edh->eth/dot_general | solution.py:63
  148.6 5.3 %fusion.27 = f32[2048,2,384]{2,0,1:T(8,128)} fusion(bf16[1,2,1024,384]{3,2,1,0:T(8,128)(2,1)S(1)} %copy-done, bf16[2048,2048]{1,0:T(8,128)(2,1)S(1)} %copy-done.3), kind=kOutput, calls=%fused_computation.45 | convolution fusion | flops 3221225472 | bytes 12058624 | tf_op jit(solution)/shard_map/td,edh->eth/dot_general | solution.py:60
  153.9 11.8 %multiply_convert_fusion.3 = (bf16[2,2048,384]{2,1,0:T(8,128)(2,1)}, bf16[2,2048,384]{2,1,0:T(8,128)(2,1)}, bf16[2,2048,384]{2,1,0:T(8,128)(2,1)S(1)}) fusion(f32[2048,2,384]{2,0,1:T(8,128)} %fusion.27, f32[2048,2,384]{2,0,1:T(8,128)} %fusion.23, bf16[1,2,384,1024]{3,2,1,0:T(8,128)(2,1)S(1)} %copy-done.7, f32[2048,1024]{1,0:T(8,128)S(1)} %slice_convert_fusion, ...), kind=kOutput, calls=%fused_computation.23 | convolution fusion | flops 3253207040 | bytes 31997952 | tf_op jit(solution)/shard_map/etd,ehd->eth/dot_general | solution.py:74
  165.7 1.6 copy-done.9
  167.3 8.7 %multiply_reduce_fusion = f32[2048,1024]{1,0:T(8,128)} fusion(f32[2,2048]{1,0:T(2,128)S(1)} %convert_bitcast_fusion, bf16[2,2048,384]{2,1,0:T(8,128)(2,1)S(1)} %get-tuple-element.23, bf16[1,2,384,1024]{3,2,1,0:T(8,128)(2,1)S(1)} %copy-done.7), kind=kOutput, calls=%fused_computation.3 | convolution fusion | flops 3235905536 | bytes 13123584 | tf_op jit(solution)/shard_map/eth,ehd->etd/dot_general | solution.py:69
  176.3 10.3 %fusion.25 = f32[2,2048,1024]{2,1,0:T(8,128)} fusion(bf16[2,2048,384]{2,1,0:T(8,128)(2,1)} %get-tuple-element.22, bf16[1,2,1024,384]{3,2,1,0:T(8,128)(2,1)S(1)} %copy-done), kind=kOutput, calls=%fused_computation.43 | convolution fusion | flops 3221225472 | bytes 21495808 | tf_op jit(solution)/shard_map/eth,edh->etd/dot_general | solution.py:89
  186.6 13.2 %convert_reduce_fusion = f32[2048,1024]{1,0:T(8,128)} fusion(f32[2,2048,1024]{2,1,0:T(8,128)} %fusion.25, bf16[2,2048,384]{2,1,0:T(8,128)(2,1)} %get-tuple-element.21, bf16[1,2,1024,384]{3,2,1,0:T(8,128)(2,1)S(1)} %copy-done.4), kind=kOutput, calls=%fused_computation | convolution fusion | flops 3235905536 | bytes 29884416 | tf_op jit(solution)/shard_map/eth,edh->etd/dot_general | solution.py:90
  199.8 1.4 copy-done.8
  201.2 1.5 collective-permute-start
  203.4 6.7 %fusion.30 = bf16[1,2,1024,384]{2,3,1,0:T(8,128)(2,1)S(1)} fusion(bf16[2,2048,384]{2,1,0:T(8,128)(2,1)} %get-tuple-element.22, bf16[2048,2048]{1,0:T(8,128)(2,1)} %all-gather.2.cloned.1.call-done), kind=kOutput, calls=%fused_computation.48 | convolution fusion | flops 3222011904 | bytes 8912896 | tf_op jit(solution)/shard_map/td,eth->edh/dot_general | solution.py:82
  210.1 1.8 copy.27
  211.9 6.7 %fusion.31 = bf16[1,2,1024,384]{2,3,1,0:T(8,128)(2,1)S(1)} fusion(bf16[2,2048,384]{2,1,0:T(8,128)(2,1)} %get-tuple-element.21, bf16[2048,2048]{1,0:T(8,128)(2,1)} %all-gather.2.cloned.1.call-done), kind=kOutput, calls=%fused_computation.49 | convolution fusion | flops 3222011904 | bytes 8912896 | tf_op jit(solution)/shard_map/td,eth->edh/dot_general | solution.py:85
  218.6 1.6 copy.28
  220.2 17.3 %collective-permute-done.1 = bf16[1,2,384,1024]{3,2,1,0:T(8,128)(2,1)} collective-permute-done((bf16[1,2,384,1024]{3,2,1,0:T(8,128)(2,1)S(1)}, bf16[1,2,384,1024]{3,2,1,0:T(8,128)(2,1)}, u32[]{:S(2)}, u32[]{:S(2)}) %collective-permute-start.1) | collective-permute-done | bytes 1572896 | tf_op jit(solution)/shard_map/ppermute | solution.py:18
  238.6 16.2 %fusion.33 = (f32[1,2,384,1024]{3,2,1,0:T(8,128)}, bf16[1,2,384,1024]{3,2,1,0:T(8,128)(2,1)}, f32[1,2,384,1024]{3,2,1,0:T(8,128)}) fusion(f32[1,2,384,1024]{3,2,1,0:T(8,128)} %param.18, f32[1,2,384,1024]{3,2,1,0:T(8,128)} %param.17, bf16[1,2,384,1024]{3,2,1,0:T(8,128)(2,1)} %collective-permute-done, bf16[1,2,384,1024]{3,2,1,0:T(8,128)(2,1)} %collective-permute-done.1, ...), kind=kOutput, calls=%fused_computation.52 | convolution fusion | flops 3246129152 | bytes 30425088 | tf_op jit(solution)/shard_map/eth,etd->ehd/dot_general | solution.py:81
  254.8 68.5 %reduce-scatter.3.cloned.1.call-done = f32[256,1024]{1,0:T(8,128)} async-done(((f32[2048,1024]{1,0:T(8,128)}), f32[256,1024]{1,0:T(8,128)}) %reduce-scatter.3.cloned.1.call-update) | async-done | bytes 1048592 | tf_op jit(solution)/shard_map/reduce_scatter | solution.py:124
  323.3 2.1 convert_element_type.69
  325.4 150.0 %reduce-scatter.5.cloned.1.call-done = f32[256,1024]{1,0:T(8,128)} async-done(((f32[2048,1024]{1,0:T(8,128)}), f32[256,1024]{1,0:T(8,128)}) %reduce-scatter.5.cloned.1.call-update) | async-done | bytes 1048592 | tf_op jit(solution)/shard_map/reduce_scatter | solution.py:127
  475.4 2.1 convert_element_type.76
  (28 shorter events, 1.5 us)
Async XLA Ops:
  7.2 141.4 %copy-start = (bf16[1,2,1024,384]{3,2,1,0:T(8,128)(2,1)S(1)}, bf16[1,2,1024,384]{3,2,1,0:T(8,128)(2,1)}, u32[]{:S(2)}) copy-start(bf16[1,2,1024,384]{3,2,1,0:T(8,128)(2,1)} %param.14) | copy-start | bytes 4718596
  7.2 2.5 copy-start.6
  7.2 2.5 copy-start.5
  7.2 131.5 %all-gather.2.cloned.1.call-start = ((), (), s32[]{:S(2)}) async-start(), calls=%async_computation.2 | async-start | bytes 9437184 | tf_op jit(solution)/shard_map/all_gather | solution.py:47
  9.7 313.7 %reduce-scatter.3.cloned.1.call-start = ((), (), s32[]{:S(2)}) async-start(), calls=%async_computation.3 | async-start | bytes 9437184 | tf_op jit(solution)/shard_map/reduce_scatter | solution.py:124
  42.5 99.6 %copy-start.4 = (bf16[1,2,1024,384]{3,2,1,0:T(8,128)(2,1)S(1)}, bf16[1,2,1024,384]{3,2,1,0:T(8,128)(2,1)}, u32[]{:S(2)}) copy-start(bf16[1,2,1024,384]{3,2,1,0:T(8,128)(2,1)} %param.15) | copy-start | bytes 4718596
  138.7 4.6 copy-start.3
  143.3 10.5 %copy-start.2 = (f32[2048,1024]{1,0:T(8,128)}, f32[2048,1024]{1,0:T(8,128)S(1)}, u32[]{:S(2)}) copy-start(f32[2048,1024]{1,0:T(8,128)S(1)} %slice_convert_fusion) | copy-start | bytes 25165828
  148.6 5.3 %copy-start.7 = (bf16[1,2,384,1024]{3,2,1,0:T(8,128)(2,1)S(1)}, bf16[1,2,384,1024]{3,2,1,0:T(8,128)(2,1)}, u32[]{:S(2)}) copy-start(bf16[1,2,384,1024]{3,2,1,0:T(8,128)(2,1)} %param.16) | copy-start | bytes 4718596
  165.7 1.6 copy-start.9
  176.1 299.3 %reduce-scatter.5.cloned.1.call-start = ((), (), s32[]{:S(2)}) async-start(), calls=%async_computation.4 | async-start | bytes 9437184 | tf_op jit(solution)/shard_map/reduce_scatter | solution.py:127
  199.8 1.5 copy-start.8
  201.2 36.2 %collective-permute-start.1 = (bf16[1,2,384,1024]{3,2,1,0:T(8,128)(2,1)S(1)}, bf16[1,2,384,1024]{3,2,1,0:T(8,128)(2,1)}, u32[]{:S(2)}, u32[]{:S(2)}) collective-permute-start(bf16[1,2,384,1024]{3,2,1,0:T(8,128)(2,1)S(1)} %copy-done.8), channel_id=1, source_target_pairs={{0,8},{8,16},{16,24},{24,0},{1,9},{9,17},{17,25},{25,1},{2,10},{10... | collective-permute-start | bytes 4718600 | tf_op jit(solution)/shard_map/ppermute | solution.py:18
  201.2 37.3 %collective-permute-start = (bf16[1,2,384,1024]{3,2,1,0:T(8,128)(2,1)S(1)}, bf16[1,2,384,1024]{3,2,1,0:T(8,128)(2,1)}, u32[]{:S(2)}, u32[]{:S(2)}) collective-permute-start(bf16[1,2,384,1024]{3,2,1,0:T(8,128)(2,1)S(1)} %copy-done.8), channel_id=1, source_target_pairs={{0,16},{8,24},{16,0},{24,8},{1,17},{9,25},{17,1},{25,9},{2,18},{10... | collective-permute-start | bytes 4718600 | tf_op jit(solution)/shard_map/ppermute | solution.py:18
  238.6 238.9 %copy-start.1 = (bf16[1,2,1024,384]{3,2,1,0:T(8,128)(2,1)S(1)}, bf16[1,2,1024,384]{3,2,1,0:T(8,128)(2,1)}, u32[]{:S(2)}) copy-start(bf16[1,2,1024,384]{3,2,1,0:T(8,128)(2,1)} %param.14) | copy-start | bytes 4718596
Sparse Core Ops, SparseCore 0:
  10.7 127.9 all-gather.1
  176.2 147.0 reduce-scatter.2
  327.4 147.9 reduce-scatter.4
